TPU v7x, 512 devices: a whole 4x4x16 slice. The times are simulated.
512 devices in a mesh: dp: 64 (over z, x), pair: 8 (over y, core).
Axes of the slice: x: 4, y: 4, z: 16, core: 2. Of those that a mesh axis runs over, the one named last changes fastest.
Arguments:
- embedding: bfloat16 [65536, 1024], P(('dp', 'pair')), may hold values from -32 to 32
- labels: int32 [65536], P(('dp', 'pair')), may hold values from 0 to 127, as said below
- order_ids: int32 [65536], P(('dp', 'pair')), may hold values from 0 to 65535, each once
Outputs:
- best_similarity: float32 [65536], P(('dp', 'pair'))
Inputs may be any that keep to these rules, and one draw needn't show every extreme that they name: `labels`: clusters 2 * g to 2 * g + 1 form owner group g. Among the 128 rows of one device (aligned blocks of the whole array) at most 4 name clusters of any one group, and in every draw some group gets exactly 4 rows from every device.
All inputs are finite; a program needn't handle non-finite values.
Results may differ from a plain program's by a relative error of at most 0.00049.
Values may be sent and summed in bfloat16 or wider, within the bound.
No kernel may reach another device: no remote copies, remote signals or barrier semaphores. Data moves between devices by JAX's collectives and lax.ppermute only.
A program may use at most 64 MiB of HBM per device.

v0:
```python
import jax
import jax.numpy as jnp
from jax import lax
from jax.sharding import PartitionSpec as P

CL_OWN = 2
META = 128
PUBLISH_ROWS = 32


def tile_best(own_rows, own_key, other_rows, other_key, rows_total):
    scores = jnp.dot(own_rows, other_rows.T, preferred_element_type=jnp.float32)
    same_cluster = other_key[None, :] // rows_total == own_key[:, None] // rows_total
    earlier = same_cluster & (other_key[None, :] < own_key[:, None])
    return jnp.max(jnp.where(earlier, scores, -1.0), axis=1)


def slot_keys(rows, width, rows_total):
    meta = rows[:, width : width + 3].astype(jnp.int32)
    return meta[:, 0] * rows_total + meta[:, 1] * 256 + meta[:, 2]


def on_device(embedding, labels, order_ids):
    groups = lax.axis_size("dp")
    pairs = lax.axis_size("pair")
    rows_here, width = embedding.shape
    rows_total = rows_here * groups * pairs
    capacity = 2 * rows_here // groups
    slot_count = groups * capacity
    values = embedding.astype(jnp.float32)
    squares = jnp.sum(values * values, axis=1, keepdims=True)
    shifted = squares + 1e-06
    unit_rows = (values * lax.rsqrt(shifted)).astype(jnp.bfloat16)
    owner_group = labels // CL_OWN
    onehot = (owner_group[:, None] == jnp.arange(groups, dtype=jnp.int32)[None, :]).astype(
        jnp.int32
    )
    before = jnp.cumsum(onehot, axis=0) - onehot
    slot_index = owner_group * capacity + jnp.sum(before * onehot, axis=1)
    meta = jnp.stack([labels + 1, order_ids // 256, order_ids % 256], axis=1).astype(jnp.bfloat16)
    meta = jnp.pad(meta, ((0, 0), (0, META - 3)))
    packed = jnp.concatenate([unit_rows, meta], axis=1)
    send_rows = jnp.zeros((slot_count, width + META), jnp.bfloat16).at[slot_index].set(packed)
    got_rows = lax.all_to_all(
        send_rows.reshape(groups, capacity, -1), "dp", split_axis=0, concat_axis=0, tiled=True
    ).reshape(slot_count, -1)
    piece_rows = lax.all_gather(got_rows, "pair", axis=0, tiled=True)
    got_key = slot_keys(got_rows, width, rows_total)
    piece_key = slot_keys(piece_rows, width, rows_total)
    column = lax.broadcasted_iota(jnp.int32, got_rows.shape, 1)
    query_rows = jnp.where(column < width, got_rows, jnp.zeros_like(got_rows))
    best_seen = jnp.full((slot_count,), -1.0, jnp.float32)
    piece_count = piece_rows.shape[0]
    for offset in range(0, piece_count, 512):
        width_now = min(512, piece_count - offset)
        found = tile_best(
            query_rows,
            got_key,
            piece_rows[offset : offset + width_now],
            piece_key[offset : offset + width_now],
            rows_total,
        )
        best_seen = jnp.maximum(best_seen, found)
    publish = jnp.zeros((PUBLISH_ROWS * 128,), jnp.float32).at[:slot_count].set(best_seen)
    published = lax.all_gather(publish.reshape(PUBLISH_ROWS, 128), "dp", axis=0, tiled=False)
    me = lax.axis_index("dp")
    answered = lax.dynamic_slice_in_dim(
        published.reshape(groups, PUBLISH_ROWS * 128), me * capacity, capacity, axis=1
    )
    return answered.reshape(slot_count)[slot_index]


def solution(mesh):
    in_specs = (P(("dp", "pair"), None), P(("dp", "pair")), P(("dp", "pair")))
    out_specs = P(("dp", "pair"))
    return jax.shard_map(
        on_device, mesh=mesh, in_specs=in_specs, out_specs=out_specs, check_vma=False
    )
```

profile of v0, /device:TPU:8, one launch (start us, length us, event | category | flops | bytes accessed | tf_op | source)
XLA Modules:
  0.0 256.4 jit_solution(14375752796550664068)
XLA Ops:
  6.5 0.0 all-gather.3.cloned.1.call-start
  6.5 0.7 convert_bitcast_fusion.1
  7.2 0.1 fusion.36
  7.3 0.2 reduce_window_sum.11
  7.5 0.2 select_reduce_fusion
  7.7 0.7 convert_bitcast_fusion
  8.3 0.1 copy.7
  8.5 1.1 fusion.18
  9.6 1.1 fusion.19
  10.6 1.3 scatter_custom_fusion
  12.0 0.1 reshape.149
  12.1 54.0 %all_to_all.5 = bf16[64,4,1152]{2,1,0:T(4,128)(2,1)S(1)} all-to-all(bf16[64,4,1152]{2,1,0:T(4,128)(2,1)S(1)} %reshape.149), channel_id=1, replica_groups=mesh['dp'=64,'pair'=8] {'dp'}, dimensions={0} | all-to-all | bytes 1179648 | tf_op jit(solution)/shard_map/all_to_all | solution.py:44
  66.1 1.0 reshape.150
  67.1 0.0 copy-start
  67.1 0.0 all-gather.3.cloned.1.call-update
  67.1 0.0 all-gather.5.cloned.1.call-start
  67.2 0.9 slice_convert_fusion.1
  68.1 0.3 fusion.33
  68.4 31.6 %all-gather.3.cloned.1.call-done = bf16[2048,1152]{1,0:T(8,128)(2,1)} async-done(((bf16[256,1152]{1,0:T(8,128)(2,1)}), bf16[2048,1152]{1,0:T(8,128)(2,1)}) %all-gather.3.cloned.1.call-update) | async-done | bytes 4718608 | tf_op jit(solution)/shard_map/all_gather | solution.py:47
  99.9 0.0 copy-start.1
  99.9 1.3 slice_convert_fusion
  101.2 0.6 slice_add_fusion
  101.8 0.4 slice_reduce_fusion.3
  102.2 0.0 copy-done
  102.2 0.2 copy-done.1
  102.4 0.6 fusion.4
  103.1 0.6 fusion.7
  103.7 0.6 fusion.10
  104.4 0.6 fusion.13
  105.0 0.6 pad_bitcast_fusion
  105.6 0.0 all-gather.5.cloned.1.call-update
  105.7 140.1 %all-gather.5.cloned.1.call-done = f32[64,32,128]{2,1,0:T(8,128)} async-done(((f32[1,32,128]{2,1,0:T(8,128)}), f32[64,32,128]{2,1,0:T(8,128)}) %all-gather.5.cloned.1.call-update) | async-done | bytes 1048592 | tf_op jit(solution)/shard_map/all_gather | solution.py:65
  245.8 1.8 copy.10
  247.6 0.1 constant_dynamic-slice_fusion
  247.7 0.1 reshape.152
  247.8 1.8 gather_fusion
  (8 shorter events, 0.1 us)
Async XLA Ops:
  6.5 93.4 %all-gather.3.cloned.1.call-start = ((), (), s32[]{:S(2)}) async-start(), calls=%async_computation.1 | async-start | bytes 5308416 | tf_op jit(solution)/shard_map/all_gather | solution.py:47
  67.1 35.1 %copy-start = (bf16[256,1152]{1,0:T(8,128)(2,1)S(1)}, bf16[256,1152]{1,0:T(8,128)(2,1)}, u32[]{:S(2)}) copy-start(bf16[256,1152]{1,0:T(8,128)(2,1)} %reshape.150) | copy-start | bytes 1769476
  67.1 178.7 %all-gather.5.cloned.1.call-start = ((), (), s32[]{:S(2)}) async-start(), calls=%async_computation.2 | async-start | bytes 1064960 | tf_op jit(solution)/shard_map/all_gather | solution.py:65
  99.9 2.5 copy-start.1
Sparse Core Ops, SparseCore 0:
  67.2 32.6 all-gather.2
  105.8 139.9 all-gather.4
where the time goes:
time: 257 us; the launch traced here: 256 us
  waiting for transfers between devices  172 us (67%)
  blocking collectives  54 us (21%)
  between operations  13.5 us (5%)
  other arithmetic  8.4 us (3%)
  local copies, waits for them, and re-layouts  6.2 us (2%)
    all_gather x1, waiting for transfers between devices, on_device(): lax.all_gather(publish.reshape(PUBLISH_ROWS, 128), 'dp', axis=0, tiled=Fa...  140 us
    all_to_all x1, blocking collectives, on_device(): lax.all_to_all(send_rows.reshape(groups, capacity, -1), 'dp', split_axis=...  54 us
    all_gather x1, waiting for transfers between devices, on_device(): piece_rows = lax.all_gather(got_rows, 'pair', axis=0, tiled=True)  31.6 us
  transfers between devices with their start and end apart: 2, of which 2 were waited for; matrix products, arithmetic and copies ran while one was open for 0% of the time, Pallas kernels for 0%

commit v1 on v0

--- a/solution.py
+++ b/solution.py
@@ -44,7 +44,26 @@
     got_rows = lax.all_to_all(
         send_rows.reshape(groups, capacity, -1), "dp", split_axis=0, concat_axis=0, tiled=True
     ).reshape(slot_count, -1)
-    piece_rows = lax.all_gather(got_rows, "pair", axis=0, tiled=True)
+    size, mine, rows_2 = (lax.axis_size("pair"), lax.axis_index("pair"), got_rows.shape[0])
+    upward = [(i, (i + 1) % size) for i in range(size)]
+    left = [(i, (i - 1) % size) for i in range(size)]
+    filled = jnp.zeros(
+        (*got_rows.shape[:0], size * rows_2, *got_rows.shape[0 + 1 :]), got_rows.dtype
+    )
+    filled = lax.dynamic_update_slice_in_dim(filled, got_rows, mine * rows_2, axis=0)
+    from_left = from_right = got_rows
+    middle = size // 2
+    for turn in range(1, middle + 1):
+        from_left = lax.ppermute(from_left, "pair", upward)
+        filled = lax.dynamic_update_slice_in_dim(
+            filled, from_left, (mine - turn) % size * rows_2, axis=0
+        )
+        if turn < size - middle:
+            from_right = lax.ppermute(from_right, "pair", left)
+            filled = lax.dynamic_update_slice_in_dim(
+                filled, from_right, (mine + turn) % size * rows_2, axis=0
+            )
+    piece_rows = filled
     got_key = slot_keys(got_rows, width, rows_total)
     piece_key = slot_keys(piece_rows, width, rows_total)
     column = lax.broadcasted_iota(jnp.int32, got_rows.shape, 1)

time: 257 us -> 258 us (level)
  waiting for transfers between devices: 172 us -> 153 us
  local copies, waits for them, and re-layouts: 6.2 us -> 17.7 us
  starting transfers between devices: 0.04 us -> 5.3 us
  matrix products: 2.55 us -> 7.48 us
    all_gather x1 -> x0, waiting for transfers between devices: 31.6 us -> none  [on_device(): piece_rows = lax.all_gather(got_rows, 'pair', axis=0, tiled=True)]
    ppermute x0 -> x7, waiting for transfers between devices: none -> 19.8 us  [the longest x4 19.8 us: on_device(): from_left = lax.ppermute(from_left, 'pair', upward)]
    dynamic_update_slice x0 -> x8, local copies, waits for them, and re-layouts: none -> 7.19 us  [the longest x4 3.63 us: on_device(): lax.dynamic_update_slice_in_dim(filled, from_left, (mine - turn) % size *...]
    all_gather x1, waiting for transfers between devices: 140 us -> 133 us  [on_device(): lax.all_gather(publish.reshape(PUBLISH_ROWS, 128), 'dp', axis=0, tiled=Fa...]
    ppermute x0 -> x7, starting transfers between devices: none -> 5.3 us  [the longest x3 5.28 us: on_device(): from_right = lax.ppermute(from_right, 'pair', left)]
    dot_general x4, matrix products: 2.55 us -> 7.48 us  [tile_best(): scores = jnp.dot(own_rows, other_rows.T, preferred_element_type=jnp.float32)]
    ppermute x0 -> x7, local copies, waits for them, and re-layouts: none -> 2.77 us  [the longest x3 1.79 us: on_device(): from_right = lax.ppermute(from_right, 'pair', left)]
    broadcast_in_dim x0 -> x1, local copies, waits for them, and re-layouts: none -> 2.72 us  [on_device(): jnp.zeros((*got_rows.shape[:0], size * rows_2, *got_rows.shape[0 + 1:]),...]
  transfers between devices with their start and end apart: 2 -> 8, of which waited for: 2 -> 5; matrix products, arithmetic and copies ran while one was open for 0% -> 5% of each run, Pallas kernels for 0% -> 0%
where the time goes in v1:
time: 258 us; the launch traced here: 257 us
  waiting for transfers between devices  153 us (59%)
  blocking collectives  54 us (21%)
  local copies, waits for them, and re-layouts  17.7 us (7%)
  between operations  13.6 us (5%)
  matrix products  7.48 us (3%)
  other arithmetic  6.4 us (2%)
  starting transfers between devices  5.3 us (2%)
    all_gather x1, waiting for transfers between devices, on_device(): lax.all_gather(publish.reshape(PUBLISH_ROWS, 128), 'dp', axis=0, tiled=Fa...  133 us
    all_to_all x1, blocking collectives, on_device(): lax.all_to_all(send_rows.reshape(groups, capacity, -1), 'dp', split_axis=...  54 us
    ppermute x4, waiting for transfers between devices, on_device(): from_left = lax.ppermute(from_left, 'pair', upward)  19.8 us
    dot_general x4, matrix products, tile_best(): scores = jnp.dot(own_rows, other_rows.T, preferred_element_type=jnp.float32)  7.48 us
    ppermute x3, starting transfers between devices, on_device(): from_right = lax.ppermute(from_right, 'pair', left)  5.28 us
  transfers between devices with their start and end apart: 8, of which 5 were waited for; matrix products, arithmetic and copies ran while one was open for 5% of the time, Pallas kernels for 0%

profile of v1, /device:TPU:8, one launch (start us, length us, event | category | flops | bytes accessed | tf_op | source)
XLA Modules:
  0.0 257.2 jit_solution(6511885523954013511)
XLA Ops:
  6.5 0.0 all-gather.2.cloned.1.call-start
  6.5 0.7 convert_bitcast_fusion.1
  7.2 0.1 fusion.35
  7.3 0.2 reduce_window_sum.11
  7.5 0.2 select_reduce_fusion
  7.7 0.7 convert_bitcast_fusion
  8.3 0.1 copy.23
  8.5 1.1 fusion.17
  9.6 1.1 fusion.18
  10.6 1.3 scatter_custom_fusion
  12.0 0.1 reshape.149
  12.1 54.0 %all_to_all.5 = bf16[64,4,1152]{2,1,0:T(4,128)(2,1)S(1)} all-to-all(bf16[64,4,1152]{2,1,0:T(4,128)(2,1)S(1)} %reshape.149), channel_id=1, replica_groups=mesh['dp'=64,'pair'=8] {'dp'}, dimensions={0} | all-to-all | bytes 1179648 | tf_op jit(solution)/shard_map/all_to_all | solution.py:44
  66.1 0.1 reshape.150
  66.3 0.0 collective-permute-start
  66.3 1.7 collective-permute-start.1
  68.0 0.2 copy.15
  68.3 7.3 %collective-permute-done = bf16[256,1152]{1,0:T(8,128)(2,1)S(1)} collective-permute-done((bf16[256,1152]{1,0:T(8,128)(2,1)S(1)}, bf16[256,1152]{1,0:T(8,128)(2,1)S(1)}, u32[]{:S(2)}, u32[]{:S(2)}) %collective-permute-start) | collective-permute-done | bytes 589856 | tf_op jit(solution)/shard_map/ppermute | solution.py:57
  75.6 0.0 collective-permute-start.2
  75.6 0.0 collective-permute-done.1
  75.6 1.8 collective-permute-start.3
  77.4 0.3 fusion.32
  77.7 2.7 %broadcast_in_dim.13 = bf16[2048,1152]{0,1:T(8,128)(2,1)} broadcast(bf16[]{:T(256)} %constant.173.clone.1), dimensions={} | broadcast | bytes 4718594 | tf_op jit(solution)/shard_map/broadcast_in_dim | solution.py:50
  80.4 0.9 constant_dynamic-update-slice_fusion.7
  81.3 0.2 copy.16
  81.5 3.4 %collective-permute-done.2 = bf16[256,1152]{1,0:T(8,128)(2,1)S(1)} collective-permute-done((bf16[256,1152]{1,0:T(8,128)(2,1)S(1)}, bf16[256,1152]{1,0:T(8,128)(2,1)S(1)}, u32[]{:S(2)}, u32[]{:S(2)}) %collective-permute-start.2) | collective-permute-done | bytes 589856 | tf_op jit(solution)/shard_map/ppermute | solution.py:57
  84.9 0.0 collective-permute-start.4
  84.9 0.9 constant_dynamic-update-slice_fusion.6
  85.8 0.2 copy.17
  86.0 0.0 collective-permute-done.3
  86.1 1.8 collective-permute-start.5
  87.8 0.9 constant_dynamic-update-slice_fusion.5
  88.7 0.2 copy.18
  89.0 0.2 copy.19
  89.2 0.9 constant_dynamic-update-slice_fusion.4
  90.2 4.0 %collective-permute-done.4 = bf16[256,1152]{1,0:T(8,128)(2,1)S(1)} collective-permute-done((bf16[256,1152]{1,0:T(8,128)(2,1)S(1)}, bf16[256,1152]{1,0:T(8,128)(2,1)S(1)}, u32[]{:S(2)}, u32[]{:S(2)}) %collective-permute-start.4) | collective-permute-done | bytes 589856 | tf_op jit(solution)/shard_map/ppermute | solution.py:57
  94.2 0.0 collective-permute-start.6
  94.2 0.9 constant_dynamic-update-slice_fusion.3
  95.1 0.2 copy.20
  95.3 0.0 collective-permute-done.5
  95.4 1.3 copy.21
  96.7 0.9 constant_dynamic-update-slice_fusion.2
  97.6 0.9 constant_dynamic-update-slice_fusion.1
  98.5 5.1 %collective-permute-done.6 = bf16[256,1152]{1,0:T(8,128)(2,1)S(1)} collective-permute-done((bf16[256,1152]{1,0:T(8,128)(2,1)S(1)}, bf16[256,1152]{1,0:T(8,128)(2,1)S(1)}, u32[]{:S(2)}, u32[]{:S(2)}) %collective-permute-start.6) | collective-permute-done | bytes 589856 | tf_op jit(solution)/shard_map/ppermute | solution.py:57
  103.5 0.2 copy.22
  103.8 0.9 constant_dynamic-update-slice_fusion
  104.7 0.8 slice_convert_fusion.1
  105.5 1.9 fusion.4
  107.3 1.9 fusion.7
  109.2 1.9 fusion.10
  111.1 1.9 fusion.13
  113.0 0.6 pad_bitcast_fusion
  113.6 0.0 all-gather.2.cloned.1.call-update
  113.6 133.0 %all-gather.2.cloned.1.call-done = f32[64,32,128]{2,1,0:T(8,128)} async-done(((f32[1,32,128]{2,1,0:T(8,128)}), f32[64,32,128]{2,1,0:T(8,128)}) %all-gather.2.cloned.1.call-update) | async-done | bytes 1048592 | tf_op jit(solution)/shard_map/all_gather | solution.py:84
  246.6 1.8 copy.26
  248.4 0.1 constant_dynamic-slice_fusion
  248.5 0.1 reshape.152
  248.6 1.8 gather_fusion
  (11 shorter events, 0.1 us)
Async XLA Ops:
  6.5 240.1 %all-gather.2.cloned.1.call-start = ((), (), s32[]{:S(2)}) async-start(), calls=%async_computation.1 | async-start | bytes 1064960 | tf_op jit(solution)/shard_map/all_gather | solution.py:84
  66.3 9.3 %collective-permute-start = (bf16[256,1152]{1,0:T(8,128)(2,1)S(1)}, bf16[256,1152]{1,0:T(8,128)(2,1)S(1)}, u32[]{:S(2)}, u32[]{:S(2)}) collective-permute-start(bf16[256,1152]{1,0:T(8,128)(2,1)S(1)} %reshape.150), channel_id=1, source_target_pairs={{0,1},{1,2},{2,3},{3,4},{4,5},{5,6},{6,7},{7,0},{8,9},{9,10},{10,1... | collective-permute-start | bytes 1769480 | tf_op jit(solution)/shard_map/ppermute | solution.py:57
  66.3 9.3 %collective-permute-start.1 = (bf16[256,1152]{1,0:T(8,128)(2,1)S(1)}, bf16[256,1152]{1,0:T(8,128)(2,1)S(1)}, u32[]{:S(2)}, u32[]{:S(2)}) collective-permute-start(bf16[256,1152]{1,0:T(8,128)(2,1)S(1)} %reshape.150), channel_id=1, source_target_pairs={{0,7},{1,0},{2,1},{3,2},{4,3},{5,4},{6,5},{7,6},{8,15},{9,8},{10,9... | collective-permute-start | bytes 1769480 | tf_op jit(solution)/shard_map/ppermute | solution.py:62
  75.6 9.3 %collective-permute-start.2 = (bf16[256,1152]{1,0:T(8,128)(2,1)S(1)}, bf16[256,1152]{1,0:T(8,128)(2,1)S(1)}, u32[]{:S(2)}, u32[]{:S(2)}) collective-permute-start(bf16[256,1152]{1,0:T(8,128)(2,1)S(1)} %collective-permute-done), channel_id=1, source_target_pairs={{0,1},{1,2},{2,3},{3,4},{4,5},{5,6},{6,7},{7,0},{8,9},{9,10},{10,1... | collective-permute-start | bytes 1769480 | tf_op jit(solution)/shard_map/ppermute | solution.py:57
  75.6 10.4 %collective-permute-start.3 = (bf16[256,1152]{1,0:T(8,128)(2,1)S(1)}, bf16[256,1152]{1,0:T(8,128)(2,1)S(1)}, u32[]{:S(2)}, u32[]{:S(2)}) collective-permute-start(bf16[256,1152]{1,0:T(8,128)(2,1)S(1)} %collective-permute-done.1), channel_id=1, source_target_pairs={{0,7},{1,0},{2,1},{3,2},{4,3},{5,4},{6,5},{7,6},{8,15},{9,8},{10,9... | collective-permute-start | bytes 1769480 | tf_op jit(solution)/shard_map/ppermute | solution.py:62
  84.9 9.3 %collective-permute-start.4 = (bf16[256,1152]{1,0:T(8,128)(2,1)S(1)}, bf16[256,1152]{1,0:T(8,128)(2,1)S(1)}, u32[]{:S(2)}, u32[]{:S(2)}) collective-permute-start(bf16[256,1152]{1,0:T(8,128)(2,1)S(1)} %collective-permute-done.2), channel_id=1, source_target_pairs={{0,1},{1,2},{2,3},{3,4},{4,5},{5,6},{6,7},{7,0},{8,9},{9,10},{10,1... | collective-permute-start | bytes 1769480 | tf_op jit(solution)/shard_map/ppermute | solution.py:57
  86.1 9.3 %collective-permute-start.5 = (bf16[256,1152]{1,0:T(8,128)(2,1)S(1)}, bf16[256,1152]{1,0:T(8,128)(2,1)}, u32[]{:S(2)}, u32[]{:S(2)}) collective-permute-start(bf16[256,1152]{1,0:T(8,128)(2,1)S(1)} %collective-permute-done.3), channel_id=1, source_target_pairs={{0,7},{1,0},{2,1},{3,2},{4,3},{5,4},{6,5},{7,6},{8,15},{9,8},{10,9... | collective-permute-start | bytes 1769480 | tf_op jit(solution)/shard_map/ppermute | solution.py:62
  94.2 9.3 %collective-permute-start.6 = (bf16[256,1152]{1,0:T(8,128)(2,1)S(1)}, bf16[256,1152]{1,0:T(8,128)(2,1)S(1)}, u32[]{:S(2)}, u32[]{:S(2)}) collective-permute-start(bf16[256,1152]{1,0:T(8,128)(2,1)S(1)} %collective-permute-done.4), channel_id=1, source_target_pairs={{0,1},{1,2},{2,3},{3,4},{4,5},{5,6},{6,7},{7,0},{8,9},{9,10},{10,1... | collective-permute-start | bytes 1769480 | tf_op jit(solution)/shard_map/ppermute | solution.py:57
Sparse Core Ops, SparseCore 0:
  113.7 132.8 all-gather.1
